TPU v7x, 32 devices: a whole 2x2x4 slice. The times are simulated.
32 devices in a mesh: tm: 2 (over x), prow: 4 (over z), pcol: 4 (over y, core).
Axes of the slice: x: 2, y: 2, z: 4, core: 2. Of those that a mesh axis runs over, the one named last changes fastest.
Arguments:
- signal: bfloat16 [2048, 15360], P(('prow', 'pcol'), 'tm'), may hold values from -8 to 8
- offsets: int32 [4], replicated, may hold values from 0 to 511, as said below
- pair_list: int32 [4, 4, 4, 2], P('prow', 'pcol'), may hold values from 0 to 3, as said below
Outputs:
- correlations: bfloat16 [4, 4, 4, 128, 128, 256], P('prow', 'pcol', None, 'tm')
Inputs may be any that keep to these rules, and one draw needn't show every extreme that they name: `offsets`: some window has the largest offset. `pair_list`: entry (a, b) of cell (r, c) pairs row block r n + a with column block b n + c, n the number of devices of pcol, and the row block's number is never above the column block's; pairs may repeat.
All inputs are finite; a program needn't handle non-finite values.
Results may differ from a plain program's by a relative error of at most 0.0058.
Values may be sent and summed in bfloat16 or wider, within the bound.
No kernel may reach another device: no remote copies, remote signals or barrier semaphores. Data moves between devices by JAX's collectives and lax.ppermute only.
A program may use at most 128 MiB of HBM per device.

v0:
```python
import math
import jax
import jax.numpy as jnp
from jax import lax
from jax.sharding import PartitionSpec as P

WIN = 7680
NF = 384
K0 = 32
LAGS = 256
SPAN = 4
NP = 4
STEP = 3840
HALO = 4352
two_pi = 2.0 * math.pi


def from_behind(value, axis, steps):
    count = lax.axis_size(axis)
    initial, last = (max(0, -steps), min(count, count - steps))
    return lax.ppermute(value, axis, [(source, source + steps) for source in range(initial, last)])


def forward_table():
    coarse = 128
    n_coarse = WIN // coarse
    freq_bins = K0 + jnp.arange(NF, dtype=jnp.int32)
    scale = two_pi / WIN
    high_idx = (jnp.arange(n_coarse, dtype=jnp.int32) * coarse)[:, None] * freq_bins[None, :] % WIN
    low_idx = jnp.arange(coarse, dtype=jnp.int32)[:, None] * freq_bins[None, :] % WIN
    high_angle = high_idx.astype(jnp.float32) * scale
    low_angle = low_idx.astype(jnp.float32) * scale
    high_cos, high_sin = (jnp.cos(high_angle)[:, None, :], jnp.sin(high_angle)[:, None, :])
    low_cos, low_sin = (jnp.cos(low_angle)[None], jnp.sin(low_angle)[None])
    cos_full = (high_cos * low_cos - high_sin * low_sin).reshape(WIN, NF)
    sin_full = (high_sin * low_cos + high_cos * low_sin).reshape(WIN, NF)
    sample_idx = jnp.arange(WIN, dtype=jnp.int32)
    taper_curve = 0.5 - 0.5 * jnp.cos(sample_idx.astype(jnp.float32) * (two_pi / WIN))
    cosine = taper_curve[:, None] * cos_full
    sine = -taper_curve[:, None] * sin_full
    return jnp.concatenate([cosine, sine], axis=1).astype(jnp.bfloat16)


def lag_table(count):
    freq_bins = K0 + jnp.arange(NF, dtype=jnp.int32)
    shifted = (jnp.arange(LAGS, dtype=jnp.int32) - LAGS // 2) % WIN
    wrapped = freq_bins[:, None] * shifted[None, :] % WIN
    phase_angle = wrapped.astype(jnp.float32) * (two_pi / WIN)
    factor = 1.0 / math.sqrt(NF * count)
    return jnp.concatenate(
        [jnp.cos(phase_angle) * factor, -jnp.sin(phase_angle) * factor], axis=0
    ).astype(jnp.bfloat16)


def whiten(spectra):
    real_part = spectra[..., :NF]
    imag_part = spectra[..., NF:]
    power_sum = real_part * real_part + imag_part * imag_part
    freq_bins = jnp.arange(NF, dtype=jnp.int32)
    band_matrix = (jnp.abs(freq_bins[:, None] - freq_bins[None, :]) <= SPAN).astype(jnp.float32)
    smooth = jnp.einsum(
        "...f,fg->...g", power_sum, band_matrix, precision=lax.Precision.HIGHEST
    ) / (2 * SPAN + 1)
    water_level = jnp.mean(power_sum, axis=-1, keepdims=True)
    weight = lax.rsqrt(smooth + 0.5 * water_level + 1e-06)
    return (spectra * jnp.concatenate([weight, weight], axis=-1)).astype(jnp.bfloat16)


def cross_pair(row_block, col_block, lags):
    row_real = row_block[..., :NF].astype(jnp.float32)[:, :, None, :]
    row_imag = row_block[..., NF:].astype(jnp.float32)[:, :, None, :]
    col_real = col_block[..., :NF].astype(jnp.float32)[:, None, :, :]
    col_imag = col_block[..., NF:].astype(jnp.float32)[:, None, :, :]
    real_sum = jnp.sum(row_real * col_real + row_imag * col_imag, axis=0)
    imag_sum = jnp.sum(row_imag * col_real - row_real * col_imag, axis=0)
    cross = jnp.concatenate([real_sum, imag_sum], axis=-1).astype(jnp.bfloat16)
    flat = cross.reshape(-1, 2 * NF)
    result = jnp.dot(flat, lags, preferred_element_type=jnp.float32).astype(jnp.bfloat16)
    return result.reshape(row_block.shape[1], col_block.shape[1], LAGS)


def on_device(signal, offsets, pair_list):
    channels_here = signal.shape[0]
    samples_here = signal.shape[1]
    w_dev = samples_here // STEP
    n_tm = lax.axis_size("tm")
    tm_index = lax.axis_index("tm")
    dft_table = forward_table()
    head_samples = signal[:, :HALO]
    next_head = from_behind(head_samples, "tm", -1)
    extended = jnp.concatenate([signal, next_head], axis=1)

    def one_window(window):
        first_sample = window * STEP + offsets[tm_index * w_dev + window]
        segment = lax.dynamic_slice_in_dim(extended, first_sample, WIN, 1)
        return jnp.dot(segment, dft_table, preferred_element_type=jnp.float32)

    spectra = lax.map(one_window, jnp.arange(w_dev, dtype=jnp.int32))
    whitened = whiten(spectra)
    own_piece = whitened[None]
    row_gathered = lax.all_gather(own_piece, ("tm", "pcol"), axis=0, tiled=True)
    col_gathered = lax.all_gather(own_piece, ("tm", "prow"), axis=0, tiled=True)
    row_gathered = row_gathered.reshape(n_tm, -1, w_dev, channels_here, 2 * NF)
    col_gathered = col_gathered.reshape(n_tm, -1, w_dev, channels_here, 2 * NF)
    pick_dim = 1
    lags = lag_table(n_tm * w_dev)
    local_pairs = pair_list[0, 0]
    half_rows = channels_here // n_tm
    first_row = tm_index * half_rows

    def one_pair(pair_index):
        row_pick = local_pairs[pair_index, 0]
        col_pick = local_pairs[pair_index, 1]
        row_whole = lax.dynamic_index_in_dim(row_gathered, row_pick, pick_dim, keepdims=False)
        col_whole = lax.dynamic_index_in_dim(col_gathered, col_pick, pick_dim, keepdims=False)
        row_whole = row_whole.reshape(n_tm * w_dev, channels_here, 2 * NF)
        col_whole = col_whole.reshape(n_tm * w_dev, channels_here, 2 * NF)
        row_block = lax.dynamic_slice_in_dim(row_whole, first_row, half_rows, 1)
        return cross_pair(row_block, col_whole, lags)

    result = lax.map(one_pair, jnp.arange(NP, dtype=jnp.int32))
    return result.reshape(1, 1, NP, half_rows, channels_here, LAGS)


def solution(mesh):
    placed = (P(("prow", "pcol"), "tm"), P(), P("prow", "pcol", None, None))
    return jax.shard_map(
        on_device,
        mesh=mesh,
        in_specs=placed,
        out_specs=P("prow", "pcol", None, "tm", None, None),
        check_vma=False,
    )
```

profile of v0, /device:TPU:0, one launch (start us, length us, event | category | flops | bytes accessed | tf_op | source)
XLA Modules:
  0.0 346.1 jit_solution(10284323201007066720)
XLA Ops:
  6.5 1.3 slice.29
  7.9 1.3 collective-permute-start
  10.8 11.8 %multiply_subtract_fusion = (f32[60,128,384]{2,1,0:T(8,128)}, f32[60,128,384]{2,1,0:T(8,128)}) fusion(f32[128,384]{1,0:T(8,128)S(1)} %get-tuple-element.241, f32[60,384]{1,0:T(8,128)S(1)} %get-tuple-element.239, f32[128,384]{1,0:T(8,128)S(1)} %get-tuple-element.240, f32[60,384]{1,0:T(8,128)S(1)} %get-tuple-element.238), kind=kLoop, calls=%fused_computation.28 | loop fusion | flops 17694720 | bytes 24170496 | tf_op jit(solution)/shard_map/sub | solution.py:35
  22.6 9.4 %fusion.17 = (bf16[7680,384]{1,0:T(8,128)(2,1)S(1)}, bf16[7680,384]{1,0:T(8,128)(2,1)S(1)}) fusion(f32[60,128,384]{2,1,0:T(8,128)} %get-tuple-element.235, f32[7680]{0:T(1024)S(1)} %fusion.46, f32[60,128,384]{2,1,0:T(8,128)} %get-tuple-element.234, f32[7680]{0:T(1024)S(1)} %multiply_subtract_fusion.1), kind=kLoop, calls=%fused_computation.24 | loop fusion | flops 11796480 | bytes 35450880 | tf_op jit(solution)/shard_map/convert.7
  32.0 5.0 %pad_maximum_fusion = bf16[7680,768]{1,0:T(8,128)(2,1)} fusion(bf16[7680,384]{1,0:T(8,128)(2,1)S(1)} %get-tuple-element.242, bf16[7680,384]{1,0:T(8,128)(2,1)S(1)} %get-tuple-element.243), kind=kLoop, calls=%fused_computation.22 | loop fusion | flops 23592960 | bytes 23592960 | tf_op jit(solution)/shard_map/concatenate | solution.py:41
  37.0 1.4 pad_maximum_fusion.1
  38.4 19.9 %while.24 = (s32[]{:T(128)}, f32[2,128,768]{2,1,0:T(8,128)}, s32[2]{0:T(128)S(1)}, s32[]{:T(128)}, s32[4]{0:T(128)S(1)}, /*index=5*/bf16[128,12032]{1,0:T(8,128)...) while((s32[]{:T(128)}, f32[2,128,768]{2,1,0:T(8,128)}, ...), condition=%wide.region_1.2_spmd, body=%wide.region_0.1_spmd.sunk | while | flops 1509949440 | bytes 14156537 | solution.py:98
  41.4 7.0 %fusion.58 = f32[2,128,768]{2,1,0:T(8,128)} fusion(f32[2,128,768]{2,1,0:T(8,128)} %get-tuple-element.369, s32[]{:T(128)} %get-tuple-element.368, bf16[7680,768]{1,0:T(8,128)(2,1)} %get-tuple-element.386, bf16[128,12032]{1,0:T(8,128)(2,1)S(1)} %get-tuple-element.385, s32[]{:T(128)S(6)} %select_n.122), kind=kOutput, calls=%fused_computation.3.clone.1 | convolution fusion | flops 1509949440 | bytes 14156292 | tf_op jit(solution)/shard_map/while/body/eval_jaxpr/dot_general | solution.py:96
  51.4 7.0 %fusion.58 = f32[2,128,768]{2,1,0:T(8,128)} fusion(f32[2,128,768]{2,1,0:T(8,128)} %get-tuple-element.369, s32[]{:T(128)} %get-tuple-element.368, bf16[7680,768]{1,0:T(8,128)(2,1)} %get-tuple-element.386, bf16[128,12032]{1,0:T(8,128)(2,1)S(1)} %get-tuple-element.385, s32[]{:T(128)S(6)} %select_n.122), kind=kOutput, calls=%fused_computation.3.clone.1 | convolution fusion | flops 1509949440 | bytes 14156292 | tf_op jit(solution)/shard_map/while/body/eval_jaxpr/dot_general | solution.py:96
  58.4 1.2 fusion.45
  59.6 1.7 fusion.21
  61.3 2.0 fusion.22
  64.1 2.0 multiply_convert_fusion.1
  66.1 34.4 %all-gather.5.cloned.1.call-done = bf16[16,128,768]{2,1,0:T(8,128)(2,1)} async-done(((bf16[2,128,768]{2,1,0:T(8,128)(2,1)}), bf16[16,128,768]{2,1,0:T(8,128)(2,1)}) %all-gather.5.cloned.1.call-update) | async-done | bytes 3145744 | tf_op jit(solution)/shard_map/all_gather | solution.py:101
  100.5 62.1 %all-gather.7.cloned.1.call-done = bf16[16,128,768]{2,1,0:T(8,128)(2,1)} async-done(((bf16[2,128,768]{2,1,0:T(8,128)(2,1)}), bf16[16,128,768]{2,1,0:T(8,128)(2,1)}) %all-gather.7.cloned.1.call-update) | async-done | bytes 3145744 | tf_op jit(solution)/shard_map/all_gather | solution.py:102
  162.6 176.7 %while.25 = (s32[]{:T(128)}, bf16[4,64,128,256]{3,2,1,0:T(8,128)(2,1)}, s32[4]{0:T(128)S(1)}, s32[4,2]{0,1:T(2,128)S(1)}, bf16[2,4,2,128,768]{4,3,2,1,0:T(8,128)...) while((s32[]{:T(128)}, ...), condition=%wide.region_6.7_spmd, body=%wide.region_3.6_spmd.sunk | while | flops 3343450112 | bytes 47186712 | solution.py:121
  169.8 1.5 constant_dynamic-slice_fusion.7
  171.5 29.1 %add_reduce_fusion.2 = (bf16[64,128,384]{2,1,0:T(8,128)(2,1)S(1)}, bf16[64,128,384]{2,1,0:T(8,128)(2,1)S(1)}) fusion(f32[4,128,384]{2,1,0:T(8,128)S(1)} %get-tuple-element.349, f32[4,64,384]{2,1,0:T(8,128)S(1)} %get-tuple-element.351, f32[4,128,384]{2,1,0:T(8,128)S(1)} %get-tuple-element.352, f32[4,64,384]{2,1,0:T(8,128)S(1)} %get-tuple-element.353), kind=kLoop, calls=%fused_computation.6.clone.1 | loop fusion | flops 94371840 | bytes 14942208 | tf_op jit(solution)/shard_map/while/body/eval_jaxpr/reduce_sum | solution.py:74
  200.6 3.9 %fusion.61 = bf16[8192,256]{1,0:T(8,128)(2,1)S(1)} fusion(bf16[768,256]{1,0:T(8,128)(2,1)S(1)} %get-tuple-element.423, bf16[8192,384]{1,0:T(8,128)(2,1)S(1)} %bitcast.62, bf16[8192,384]{1,0:T(8,128)(2,1)S(1)} %bitcast.61), kind=kOutput, calls=%fused_computation.11.clone.1 | convolution fusion | flops 3248488448 | bytes 17170432 | tf_op jit(solution)/shard_map/while/body/eval_jaxpr/dot_general | solution.py:78
  204.5 2.3 constant_dynamic-update-slice_fusion.2
  214.0 1.5 constant_dynamic-slice_fusion.7
  215.6 29.1 %add_reduce_fusion.2 = (bf16[64,128,384]{2,1,0:T(8,128)(2,1)S(1)}, bf16[64,128,384]{2,1,0:T(8,128)(2,1)S(1)}) fusion(f32[4,128,384]{2,1,0:T(8,128)S(1)} %get-tuple-element.349, f32[4,64,384]{2,1,0:T(8,128)S(1)} %get-tuple-element.351, f32[4,128,384]{2,1,0:T(8,128)S(1)} %get-tuple-element.352, f32[4,64,384]{2,1,0:T(8,128)S(1)} %get-tuple-element.353), kind=kLoop, calls=%fused_computation.6.clone.1 | loop fusion | flops 94371840 | bytes 14942208 | tf_op jit(solution)/shard_map/while/body/eval_jaxpr/reduce_sum | solution.py:74
  244.7 3.9 %fusion.61 = bf16[8192,256]{1,0:T(8,128)(2,1)S(1)} fusion(bf16[768,256]{1,0:T(8,128)(2,1)S(1)} %get-tuple-element.423, bf16[8192,384]{1,0:T(8,128)(2,1)S(1)} %bitcast.62, bf16[8192,384]{1,0:T(8,128)(2,1)S(1)} %bitcast.61), kind=kOutput, calls=%fused_computation.11.clone.1 | convolution fusion | flops 3248488448 | bytes 17170432 | tf_op jit(solution)/shard_map/while/body/eval_jaxpr/dot_general | solution.py:78
  248.7 2.3 constant_dynamic-update-slice_fusion.2
  258.1 1.5 constant_dynamic-slice_fusion.7
  259.8 29.1 %add_reduce_fusion.2 = (bf16[64,128,384]{2,1,0:T(8,128)(2,1)S(1)}, bf16[64,128,384]{2,1,0:T(8,128)(2,1)S(1)}) fusion(f32[4,128,384]{2,1,0:T(8,128)S(1)} %get-tuple-element.349, f32[4,64,384]{2,1,0:T(8,128)S(1)} %get-tuple-element.351, f32[4,128,384]{2,1,0:T(8,128)S(1)} %get-tuple-element.352, f32[4,64,384]{2,1,0:T(8,128)S(1)} %get-tuple-element.353), kind=kLoop, calls=%fused_computation.6.clone.1 | loop fusion | flops 94371840 | bytes 14942208 | tf_op jit(solution)/shard_map/while/body/eval_jaxpr/reduce_sum | solution.py:74
  288.9 3.9 %fusion.61 = bf16[8192,256]{1,0:T(8,128)(2,1)S(1)} fusion(bf16[768,256]{1,0:T(8,128)(2,1)S(1)} %get-tuple-element.423, bf16[8192,384]{1,0:T(8,128)(2,1)S(1)} %bitcast.62, bf16[8192,384]{1,0:T(8,128)(2,1)S(1)} %bitcast.61), kind=kOutput, calls=%fused_computation.11.clone.1 | convolution fusion | flops 3248488448 | bytes 17170432 | tf_op jit(solution)/shard_map/while/body/eval_jaxpr/dot_general | solution.py:78
  292.8 2.3 constant_dynamic-update-slice_fusion.2
  302.3 1.5 constant_dynamic-slice_fusion.7
  304.0 29.1 %add_reduce_fusion.2 = (bf16[64,128,384]{2,1,0:T(8,128)(2,1)S(1)}, bf16[64,128,384]{2,1,0:T(8,128)(2,1)S(1)}) fusion(f32[4,128,384]{2,1,0:T(8,128)S(1)} %get-tuple-element.349, f32[4,64,384]{2,1,0:T(8,128)S(1)} %get-tuple-element.351, f32[4,128,384]{2,1,0:T(8,128)S(1)} %get-tuple-element.352, f32[4,64,384]{2,1,0:T(8,128)S(1)} %get-tuple-element.353), kind=kLoop, calls=%fused_computation.6.clone.1 | loop fusion | flops 94371840 | bytes 14942208 | tf_op jit(solution)/shard_map/while/body/eval_jaxpr/reduce_sum | solution.py:74
  333.1 3.9 %fusion.61 = bf16[8192,256]{1,0:T(8,128)(2,1)S(1)} fusion(bf16[768,256]{1,0:T(8,128)(2,1)S(1)} %get-tuple-element.423, bf16[8192,384]{1,0:T(8,128)(2,1)S(1)} %bitcast.62, bf16[8192,384]{1,0:T(8,128)(2,1)S(1)} %bitcast.61), kind=kOutput, calls=%fused_computation.11.clone.1 | convolution fusion | flops 3248488448 | bytes 17170432 | tf_op jit(solution)/shard_map/while/body/eval_jaxpr/dot_general | solution.py:78
  337.0 2.3 constant_dynamic-update-slice_fusion.2
  (44 shorter events, 10.8 us)
Async XLA Ops:
  6.5 93.9 %all-gather.5.cloned.1.call-start = ((), (), s32[]{:S(2)}) async-start(), calls=%async_computation | async-start | bytes 3538944 | tf_op jit(solution)/shard_map/all_gather | solution.py:101
  7.9 29.1 %collective-permute-start = (bf16[128,4352]{1,0:T(8,128)(2,1)S(1)}, bf16[128,4352]{1,0:T(8,128)(2,1)}, u32[]{:S(2)}, u32[]{:S(2)}) collective-permute-start(bf16[128,4352]{1,0:T(8,128)(2,1)S(1)} %slice.29), channel_id=1, source_target_pairs={{16,0},{17,1},{18,2},{19,3},{20,4},{21,5},{22,6},{23,7},{24,8},{25... | collective-permute-start | bytes 3342344 | tf_op jit(solution)/shard_map/ppermute | solution.py:21
  32.0 5.0 %copy-start = (bf16[128,7680]{1,0:T(8,128)(2,1)S(1)}, bf16[128,7680]{1,0:T(8,128)(2,1)}, u32[]{:S(2)}) copy-start(bf16[128,7680]{1,0:T(8,128)(2,1)} %param.7) | copy-start | bytes 5898244
  32.0 6.4 %copy-start.2 = (s32[4]{0:T(128)S(1)}, s32[4]{0:T(128)}, u32[]{:S(2)}) copy-start(s32[4]{0:T(128)} %param.8) | copy-start | bytes 52
  38.4 124.2 %copy-start.1 = (s32[1,1,4,2]{2,3,1,0:T(2,128)S(1)}, s32[1,1,4,2]{2,3,1,0:T(2,128)}, u32[]{:S(2)}) copy-start(s32[1,1,4,2]{2,3,1,0:T(2,128)} %param.9) | copy-start | bytes 100
  63.3 99.3 %all-gather.7.cloned.1.call-start = ((), (), s32[]{:S(2)}) async-start(), calls=%async_computation.1 | async-start | bytes 3538944 | tf_op jit(solution)/shard_map/all_gather | solution.py:102
Sparse Core Ops, SparseCore 0:
  63.4 36.9 all-gather.4
  102.6 60.0 all-gather.6
where the time goes:
time: 347 us; the launch traced here: 346 us
  other arithmetic  151 us (44%)
  waiting for transfers between devices  97.1 us (28%)
  matrix products  31.3 us (9%)
  loops' own time  27 us (8%)
  local copies, waits for them, and re-layouts  24.2 us (7%)
  between operations  13.5 us (4%)
    reduce_sum x4, other arithmetic, cross_pair(): real_sum = jnp.sum(row_real * col_real + row_imag * col_imag, axis=0)  116 us
    all_gather x1, waiting for transfers between devices, on_device(): col_gathered = lax.all_gather(own_piece, ('tm', 'prow'), axis=0, tiled=True)  62.1 us
    all_gather x1, waiting for transfers between devices, on_device(): row_gathered = lax.all_gather(own_piece, ('tm', 'pcol'), axis=0, tiled=True)  34.4 us
    another operation x1, loops' own time, on_device(): result = lax.map(one_pair, jnp.arange(NP, dtype=jnp.int32))  23.5 us
    dot_general x4, matrix products, cross_pair(): jnp.dot(flat, lags, preferred_element_type=jnp.float32).astype(jnp.bfloat16)  15.7 us
    dot_general x2, matrix products, one_window(): return jnp.dot(segment, dft_table, preferred_element_type=jnp.float32)  14 us
    sub x1, other arithmetic, forward_table(): cos_full = (high_cos * low_cos - high_sin * low_sin).reshape(WIN, NF)  11.8 us
    another operation x2, other arithmetic  11.3 us
  transfers between devices with their start and end apart: 3, of which 2 were waited for; matrix products, arithmetic and copies ran while one was open for 9% of the time, Pallas kernels for 0%

commit v1 on v0

--- a/solution.py
+++ b/solution.py
@@ -13,6 +13,27 @@
 STEP = 3840
 HALO = 4352
 two_pi = 2.0 * math.pi
+
+
+def ring_gather(array, axis, dim):
+    peers, index, span = (lax.axis_size(axis), lax.axis_index(axis), array.shape[dim])
+    upward = [(i, (i + 1) % peers) for i in range(peers)]
+    left = [(i, (i - 1) % peers) for i in range(peers)]
+    out = jnp.zeros((*array.shape[:dim], peers * span, *array.shape[dim + 1 :]), array.dtype)
+    out = lax.dynamic_update_slice_in_dim(out, array, index * span, axis=dim)
+    from_left = from_right = array
+    halfway = peers // 2
+    for step in range(1, halfway + 1):
+        from_left = lax.ppermute(from_left, axis, upward)
+        out = lax.dynamic_update_slice_in_dim(
+            out, from_left, (index - step) % peers * span, axis=dim
+        )
+        if step < peers - halfway:
+            from_right = lax.ppermute(from_right, axis, left)
+            out = lax.dynamic_update_slice_in_dim(
+                out, from_right, (index + step) % peers * span, axis=dim
+            )
+    return out
 
 
 def from_behind(value, axis, steps):
@@ -99,7 +120,7 @@
     whitened = whiten(spectra)
     own_piece = whitened[None]
     row_gathered = lax.all_gather(own_piece, ("tm", "pcol"), axis=0, tiled=True)
-    col_gathered = lax.all_gather(own_piece, ("tm", "prow"), axis=0, tiled=True)
+    col_gathered = ring_gather(own_piece, ("tm", "prow"), 0)
     row_gathered = row_gathered.reshape(n_tm, -1, w_dev, channels_here, 2 * NF)
     col_gathered = col_gathered.reshape(n_tm, -1, w_dev, channels_here, 2 * NF)
     pick_dim = 1

time: 347 us -> 320 us (0.922)
  waiting for transfers between devices: 97.1 us -> 40.3 us
  starting transfers between devices: 1.52 us -> 21 us
  local copies, waits for them, and re-layouts: 24.2 us -> 34.2 us
    all_gather x1 -> x0, waiting for transfers between devices: 62.1 us -> none  [on_device(): col_gathered = lax.all_gather(own_piece, ('tm', 'prow'), axis=0, tiled=True)]
    ppermute x0 -> x7, waiting for transfers between devices: none -> 40.3 us  [the longest x4 33.7 us: ring_gather(): from_left = lax.ppermute(from_left, axis, upward)]
    all_gather x1, waiting for transfers between devices: 34.4 us -> 0.02 us  [on_device(): row_gathered = lax.all_gather(own_piece, ('tm', 'pcol'), axis=0, tiled=True)]
    ppermute x0 -> x7, starting transfers between devices: none -> 19.7 us  [the longest x3 16.6 us: ring_gather(): from_right = lax.ppermute(from_right, axis, left)]
    dynamic_update_slice x0 -> x7, local copies, waits for them, and re-layouts: none -> 5.18 us  [the longest x4 3.1 us: ring_gather(): lax.dynamic_update_slice_in_dim(out, from_left, (index - step) % peers *...]
    while x0 -> x24, local copies, waits for them, and re-layouts: none -> 3.97 us
  transfers between devices with their start and end apart: 3 -> 9, of which waited for: 2 -> 7; matrix products, arithmetic and copies ran while one was open for 9% -> 11% of each run, Pallas kernels for 0% -> 0%
where the time goes in v1:
time: 320 us; the launch traced here: 318 us
  other arithmetic  152 us (48%)
  waiting for transfers between devices  40.3 us (13%)
  local copies, waits for them, and re-layouts  34.2 us (11%)
  matrix products  31.3 us (10%)
  loops' own time  25.6 us (8%)
  starting transfers between devices  21 us (7%)
  between operations  13.7 us (4%)
    reduce_sum x4, other arithmetic, cross_pair(): real_sum = jnp.sum(row_real * col_real + row_imag * col_imag, axis=0)  116 us
    ppermute x4, waiting for transfers between devices, ring_gather(): from_left = lax.ppermute(from_left, axis, upward)  33.7 us
    another operation x1, loops' own time, on_device(): result = lax.map(one_pair, jnp.arange(NP, dtype=jnp.int32))  21.8 us
    ppermute x3, starting transfers between devices, ring_gather(): from_right = lax.ppermute(from_right, axis, left)  16.6 us
    dot_general x4, matrix products, cross_pair(): jnp.dot(flat, lags, preferred_element_type=jnp.float32).astype(jnp.bfloat16)  15.7 us
    dot_general x2, matrix products, one_window(): return jnp.dot(segment, dft_table, preferred_element_type=jnp.float32)  13.9 us
    sub x1, other arithmetic, forward_table(): cos_full = (high_cos * low_cos - high_sin * low_sin).reshape(WIN, NF)  11.8 us
    another operation x2, other arithmetic  11.3 us
  transfers between devices with their start and end apart: 9, of which 7 were waited for; matrix products, arithmetic and copies ran while one was open for 11% of the time, Pallas kernels for 0%

profile of v1, /device:TPU:0, one launch (start us, length us, event | category | flops | bytes accessed | tf_op | source)
XLA Modules:
  0.0 318.4 jit_solution(6366023684613794909)
XLA Ops:
  10.8 11.8 %multiply_subtract_fusion = (f32[60,128,384]{2,1,0:T(8,128)}, f32[60,128,384]{2,1,0:T(8,128)}) fusion(f32[128,384]{1,0:T(8,128)S(1)} %get-tuple-element.251, f32[60,384]{1,0:T(8,128)S(1)} %get-tuple-element.249, f32[128,384]{1,0:T(8,128)S(1)} %get-tuple-element.250, f32[60,384]{1,0:T(8,128)S(1)} %get-tuple-element.248), kind=kLoop, calls=%fused_computation.28 | loop fusion | flops 17694720 | bytes 24170496 | tf_op jit(solution)/shard_map/sub | solution.py:56
  22.6 9.4 %fusion.17 = (bf16[7680,384]{1,0:T(8,128)(2,1)S(1)}, bf16[7680,384]{1,0:T(8,128)(2,1)S(1)}) fusion(f32[60,128,384]{2,1,0:T(8,128)} %get-tuple-element.245, f32[7680]{0:T(1024)S(1)} %fusion.46, f32[60,128,384]{2,1,0:T(8,128)} %get-tuple-element.244, f32[7680]{0:T(1024)S(1)} %multiply_subtract_fusion.1), kind=kLoop, calls=%fused_computation.24 | loop fusion | flops 11796480 | bytes 35450880 | tf_op jit(solution)/shard_map/convert.7
  32.0 5.0 %pad_maximum_fusion = bf16[7680,768]{1,0:T(8,128)(2,1)} fusion(bf16[7680,384]{1,0:T(8,128)(2,1)S(1)} %get-tuple-element.252, bf16[7680,384]{1,0:T(8,128)(2,1)S(1)} %get-tuple-element.253), kind=kLoop, calls=%fused_computation.22 | loop fusion | flops 23592960 | bytes 23592960 | tf_op jit(solution)/shard_map/concatenate | solution.py:62
  38.4 20.3 %while.24 = (s32[]{:T(128)}, f32[2,128,768]{2,1,0:T(8,128)}, s32[2]{0:T(128)S(1)}, s32[]{:T(128)}, s32[4]{0:T(128)S(1)}, /*index=5*/bf16[128,12032]{1,0:T(8,128)...) while((s32[]{:T(128)}, f32[2,128,768]{2,1,0:T(8,128)}, ...), condition=%wide.region_1.2_spmd, body=%wide.region_0.1_spmd.sunk | while | flops 1509949440 | bytes 14156537 | solution.py:119
  41.6 7.0 %fusion.59 = f32[2,128,768]{2,1,0:T(8,128)} fusion(f32[2,128,768]{2,1,0:T(8,128)} %get-tuple-element.379, s32[]{:T(128)} %get-tuple-element.378, bf16[7680,768]{1,0:T(8,128)(2,1)} %get-tuple-element.396, bf16[128,12032]{1,0:T(8,128)(2,1)S(1)} %get-tuple-element.395, s32[]{:T(128)S(6)} %select_n.191), kind=kOutput, calls=%fused_computation.3.clone.1 | convolution fusion | flops 1509949440 | bytes 14156292 | tf_op jit(solution)/shard_map/while/body/eval_jaxpr/dot_general | solution.py:117
  51.8 6.9 %fusion.59 = f32[2,128,768]{2,1,0:T(8,128)} fusion(f32[2,128,768]{2,1,0:T(8,128)} %get-tuple-element.379, s32[]{:T(128)} %get-tuple-element.378, bf16[7680,768]{1,0:T(8,128)(2,1)} %get-tuple-element.396, bf16[128,12032]{1,0:T(8,128)(2,1)S(1)} %get-tuple-element.395, s32[]{:T(128)S(6)} %select_n.191), kind=kOutput, calls=%fused_computation.3.clone.1 | convolution fusion | flops 1509949440 | bytes 14156292 | tf_op jit(solution)/shard_map/while/body/eval_jaxpr/dot_general | solution.py:117
  60.0 1.7 fusion.21
  62.0 2.0 constant_dynamic-update-slice_fusion.8
  64.0 3.1 collective-permute-start.1
  67.1 5.1 %collective-permute-start.2 = (bf16[1,2,128,768]{3,2,1,0:T(8,128)(2,1)}, bf16[1,2,128,768]{3,2,1,0:T(8,128)(2,1)}, u32[]{:S(2)}, u32[]{:S(2)}) collective-permute-start(bf16[1,2,128,768]{3,2,1,0:T(8,128)(2,1)} %bitcast.71), channel_id=1, source_target_pairs={{0,28},{4,0},{8,4},{12,8},{16,12},{20,16},{24,20},{28,24},{1,29},{... | collective-permute-start | bytes 1179656 | tf_op jit(solution)/shard_map/ppermute | solution.py:32
  72.2 10.2 %collective-permute-done.1 = bf16[1,2,128,768]{3,2,1,0:T(8,128)(2,1)S(1)} collective-permute-done((bf16[1,2,128,768]{3,2,1,0:T(8,128)(2,1)}, bf16[1,2,128,768]{3,2,1,0:T(8,128)(2,1)S(1)}, u32[]{:S(2)}, u32[]{:S(2)}) %collective-permute-start.1) | collective-permute-done | bytes 393248 | tf_op jit(solution)/shard_map/ppermute | solution.py:27
  82.4 4.0 %collective-permute-done.2 = bf16[1,2,128,768]{3,2,1,0:T(8,128)(2,1)} collective-permute-done((bf16[1,2,128,768]{3,2,1,0:T(8,128)(2,1)}, bf16[1,2,128,768]{3,2,1,0:T(8,128)(2,1)}, u32[]{:S(2)}, u32[]{:S(2)}) %collective-permute-start.2) | collective-permute-done | bytes 393248 | tf_op jit(solution)/shard_map/ppermute | solution.py:32
  86.4 4.2 %collective-permute-start.4 = (bf16[1,2,128,768]{3,2,1,0:T(8,128)(2,1)}, bf16[1,2,128,768]{3,2,1,0:T(8,128)(2,1)}, u32[]{:S(2)}, u32[]{:S(2)}) collective-permute-start(bf16[1,2,128,768]{3,2,1,0:T(8,128)(2,1)} %collective-permute-done.2), channel_id=1, source_target_pairs={{0,28},{4,0},{8,4},{12,8},{16,12},{20,16},{24,20},{28,24},{1,29},{... | collective-permute-start | bytes 1179656 | tf_op jit(solution)/shard_map/ppermute | solution.py:32
  90.6 9.9 %collective-permute-done.3 = bf16[1,2,128,768]{3,2,1,0:T(8,128)(2,1)} collective-permute-done((bf16[1,2,128,768]{3,2,1,0:T(8,128)(2,1)S(1)}, bf16[1,2,128,768]{3,2,1,0:T(8,128)(2,1)}, u32[]{:S(2)}, u32[]{:S(2)}) %collective-permute-start.3) | collective-permute-done | bytes 393248 | tf_op jit(solution)/shard_map/ppermute | solution.py:27
  100.5 1.9 multiply_convert_fusion.1
  104.8 7.3 %collective-permute-start.6 = (bf16[1,2,128,768]{3,2,1,0:T(8,128)(2,1)}, bf16[1,2,128,768]{3,2,1,0:T(8,128)(2,1)S(1)}, u32[]{:S(2)}, u32[]{:S(2)}) collective-permute-start(bf16[1,2,128,768]{3,2,1,0:T(8,128)(2,1)} %collective-permute-done.4), channel_id=1, source_target_pairs={{0,28},{4,0},{8,4},{12,8},{16,12},{20,16},{24,20},{28,24},{1,29},{... | collective-permute-start | bytes 1179656 | tf_op jit(solution)/shard_map/ppermute | solution.py:32
  113.2 5.3 %collective-permute-done.5 = bf16[1,2,128,768]{3,2,1,0:T(8,128)(2,1)} collective-permute-done((bf16[1,2,128,768]{3,2,1,0:T(8,128)(2,1)}, bf16[1,2,128,768]{3,2,1,0:T(8,128)(2,1)}, u32[]{:S(2)}, u32[]{:S(2)}) %collective-permute-start.5) | collective-permute-done | bytes 393248 | tf_op jit(solution)/shard_map/ppermute | solution.py:27
  121.5 2.1 collective-permute-done.6
  123.6 8.4 %collective-permute-done.7 = bf16[1,2,128,768]{3,2,1,0:T(8,128)(2,1)S(1)} collective-permute-done((bf16[1,2,128,768]{3,2,1,0:T(8,128)(2,1)}, bf16[1,2,128,768]{3,2,1,0:T(8,128)(2,1)S(1)}, u32[]{:S(2)}, u32[]{:S(2)}) %collective-permute-start.7) | collective-permute-done | bytes 393248 | tf_op jit(solution)/shard_map/ppermute | solution.py:27
  132.1 179.4 %while.25 = (s32[]{:T(128)}, bf16[4,64,128,256]{3,2,1,0:T(8,128)(2,1)}, s32[4]{0:T(128)S(1)}, s32[4,2]{0,1:T(2,128)S(1)}, bf16[2,4,2,128,768]{4,3,2,1,0:T(8,128)...) while((s32[]{:T(128)}, ...), condition=%wide.region_6.7_spmd, body=%wide.region_3.6_spmd.sunk | while | flops 3343450112 | bytes 73925488 | solution.py:142
  140.6 29.1 %add_reduce_fusion.2 = (bf16[64,128,384]{2,1,0:T(8,128)(2,1)S(1)}, bf16[64,128,384]{2,1,0:T(8,128)(2,1)S(1)}) fusion(f32[4,128,384]{2,1,0:T(8,128)S(1)} %get-tuple-element.359, f32[4,64,384]{2,1,0:T(8,128)S(1)} %get-tuple-element.361, f32[4,128,384]{2,1,0:T(8,128)S(1)} %get-tuple-element.362, f32[4,64,384]{2,1,0:T(8,128)S(1)} %get-tuple-element.363), kind=kLoop, calls=%fused_computation.6.clone.1 | loop fusion | flops 94371840 | bytes 14942208 | tf_op jit(solution)/shard_map/while/body/eval_jaxpr/reduce_sum | solution.py:95
  169.7 3.9 %fusion.62 = bf16[8192,256]{1,0:T(8,128)(2,1)S(1)} fusion(bf16[768,256]{1,0:T(8,128)(2,1)S(1)} %copy-done.3, bf16[8192,384]{1,0:T(8,128)(2,1)S(1)} %bitcast.64, bf16[8192,384]{1,0:T(8,128)(2,1)S(1)} %bitcast.63), kind=kOutput, calls=%fused_computation.11.clone.1 | convolution fusion | flops 3248488448 | bytes 17170432 | tf_op jit(solution)/shard_map/while/body/eval_jaxpr/dot_general | solution.py:99
  173.6 2.4 constant_dynamic-update-slice_fusion.10
  185.4 29.1 %add_reduce_fusion.2 = (bf16[64,128,384]{2,1,0:T(8,128)(2,1)S(1)}, bf16[64,128,384]{2,1,0:T(8,128)(2,1)S(1)}) fusion(f32[4,128,384]{2,1,0:T(8,128)S(1)} %get-tuple-element.359, f32[4,64,384]{2,1,0:T(8,128)S(1)} %get-tuple-element.361, f32[4,128,384]{2,1,0:T(8,128)S(1)} %get-tuple-element.362, f32[4,64,384]{2,1,0:T(8,128)S(1)} %get-tuple-element.363), kind=kLoop, calls=%fused_computation.6.clone.1 | loop fusion | flops 94371840 | bytes 14942208 | tf_op jit(solution)/shard_map/while/body/eval_jaxpr/reduce_sum | solution.py:95
  214.5 3.9 %fusion.62 = bf16[8192,256]{1,0:T(8,128)(2,1)S(1)} fusion(bf16[768,256]{1,0:T(8,128)(2,1)S(1)} %copy-done.3, bf16[8192,384]{1,0:T(8,128)(2,1)S(1)} %bitcast.64, bf16[8192,384]{1,0:T(8,128)(2,1)S(1)} %bitcast.63), kind=kOutput, calls=%fused_computation.11.clone.1 | convolution fusion | flops 3248488448 | bytes 17170432 | tf_op jit(solution)/shard_map/while/body/eval_jaxpr/dot_general | solution.py:99
  218.5 2.4 constant_dynamic-update-slice_fusion.10
  230.3 29.1 %add_reduce_fusion.2 = (bf16[64,128,384]{2,1,0:T(8,128)(2,1)S(1)}, bf16[64,128,384]{2,1,0:T(8,128)(2,1)S(1)}) fusion(f32[4,128,384]{2,1,0:T(8,128)S(1)} %get-tuple-element.359, f32[4,64,384]{2,1,0:T(8,128)S(1)} %get-tuple-element.361, f32[4,128,384]{2,1,0:T(8,128)S(1)} %get-tuple-element.362, f32[4,64,384]{2,1,0:T(8,128)S(1)} %get-tuple-element.363), kind=kLoop, calls=%fused_computation.6.clone.1 | loop fusion | flops 94371840 | bytes 14942208 | tf_op jit(solution)/shard_map/while/body/eval_jaxpr/reduce_sum | solution.py:95
  259.4 3.9 %fusion.62 = bf16[8192,256]{1,0:T(8,128)(2,1)S(1)} fusion(bf16[768,256]{1,0:T(8,128)(2,1)S(1)} %copy-done.3, bf16[8192,384]{1,0:T(8,128)(2,1)S(1)} %bitcast.64, bf16[8192,384]{1,0:T(8,128)(2,1)S(1)} %bitcast.63), kind=kOutput, calls=%fused_computation.11.clone.1 | convolution fusion | flops 3248488448 | bytes 17170432 | tf_op jit(solution)/shard_map/while/body/eval_jaxpr/dot_general | solution.py:99
  263.3 2.4 constant_dynamic-update-slice_fusion.10
  275.1 29.1 %add_reduce_fusion.2 = (bf16[64,128,384]{2,1,0:T(8,128)(2,1)S(1)}, bf16[64,128,384]{2,1,0:T(8,128)(2,1)S(1)}) fusion(f32[4,128,384]{2,1,0:T(8,128)S(1)} %get-tuple-element.359, f32[4,64,384]{2,1,0:T(8,128)S(1)} %get-tuple-element.361, f32[4,128,384]{2,1,0:T(8,128)S(1)} %get-tuple-element.362, f32[4,64,384]{2,1,0:T(8,128)S(1)} %get-tuple-element.363), kind=kLoop, calls=%fused_computation.6.clone.1 | loop fusion | flops 94371840 | bytes 14942208 | tf_op jit(solution)/shard_map/while/body/eval_jaxpr/reduce_sum | solution.py:95
  304.2 3.9 %fusion.62 = bf16[8192,256]{1,0:T(8,128)(2,1)S(1)} fusion(bf16[768,256]{1,0:T(8,128)(2,1)S(1)} %copy-done.3, bf16[8192,384]{1,0:T(8,128)(2,1)S(1)} %bitcast.64, bf16[8192,384]{1,0:T(8,128)(2,1)S(1)} %bitcast.63), kind=kOutput, calls=%fused_computation.11.clone.1 | convolution fusion | flops 3248488448 | bytes 17170432 | tf_op jit(solution)/shard_map/while/body/eval_jaxpr/dot_general | solution.py:99
  308.2 2.4 constant_dynamic-update-slice_fusion.10
  (89 shorter events, 32.1 us)
Async XLA Ops:
  6.5 125.6 %all-gather.3.cloned.1.call-start = ((), (), s32[]{:S(2)}) async-start(), calls=%async_computation | async-start | bytes 3538944 | tf_op jit(solution)/shard_map/all_gather | solution.py:122
  7.9 29.1 %collective-permute-start = (bf16[128,4352]{1,0:T(8,128)(2,1)S(1)}, bf16[128,4352]{1,0:T(8,128)(2,1)}, u32[]{:S(2)}, u32[]{:S(2)}) collective-permute-start(bf16[128,4352]{1,0:T(8,128)(2,1)S(1)} %slice.29), channel_id=1, source_target_pairs={{16,0},{17,1},{18,2},{19,3},{20,4},{21,5},{22,6},{23,7},{24,8},{25... | collective-permute-start | bytes 3342344 | tf_op jit(solution)/shard_map/ppermute | solution.py:42
  32.0 5.0 %copy-start.2 = (bf16[128,7680]{1,0:T(8,128)(2,1)S(1)}, bf16[128,7680]{1,0:T(8,128)(2,1)}, u32[]{:S(2)}) copy-start(bf16[128,7680]{1,0:T(8,128)(2,1)} %param.7) | copy-start | bytes 5898244
  32.0 6.4 %copy-start.6 = (s32[4]{0:T(128)S(1)}, s32[4]{0:T(128)}, u32[]{:S(2)}) copy-start(s32[4]{0:T(128)} %param.8) | copy-start | bytes 52
  61.7 70.5 %copy-start.5 = (s32[1,1,4,2]{2,3,1,0:T(2,128)S(1)}, s32[1,1,4,2]{2,3,1,0:T(2,128)}, u32[]{:S(2)}) copy-start(s32[1,1,4,2]{2,3,1,0:T(2,128)} %param.9) | copy-start | bytes 100
  64.0 18.4 %collective-permute-start.1 = (bf16[1,2,128,768]{3,2,1,0:T(8,128)(2,1)}, bf16[1,2,128,768]{3,2,1,0:T(8,128)(2,1)S(1)}, u32[]{:S(2)}, u32[]{:S(2)}) collective-permute-start(bf16[1,2,128,768]{3,2,1,0:T(8,128)(2,1)} %bitcast.70), channel_id=1, source_target_pairs={{0,4},{4,8},{8,12},{12,16},{16,20},{20,24},{24,28},{28,0},{1,5},{5... | collective-permute-start | bytes 1179656 | tf_op jit(solution)/shard_map/ppermute | solution.py:27
  67.1 19.3 %collective-permute-start.2 = (bf16[1,2,128,768]{3,2,1,0:T(8,128)(2,1)}, bf16[1,2,128,768]{3,2,1,0:T(8,128)(2,1)}, u32[]{:S(2)}, u32[]{:S(2)}) collective-permute-start(bf16[1,2,128,768]{3,2,1,0:T(8,128)(2,1)} %bitcast.71), channel_id=1, source_target_pairs={{0,28},{4,0},{8,4},{12,8},{16,12},{20,16},{24,20},{28,24},{1,29},{... | collective-permute-start | bytes 1179656 | tf_op jit(solution)/shard_map/ppermute | solution.py:32
  82.4 18.1 %copy-start.4 = (bf16[1,2,128,768]{3,2,1,0:T(8,128)(2,1)}, bf16[1,2,128,768]{3,2,1,0:T(8,128)(2,1)S(1)}, u32[]{:S(2)}) copy-start(bf16[1,2,128,768]{3,2,1,0:T(8,128)(2,1)S(1)} %collective-permute-done.1) | copy-start | bytes 1179652
  82.4 18.1 %collective-permute-start.3 = (bf16[1,2,128,768]{3,2,1,0:T(8,128)(2,1)S(1)}, bf16[1,2,128,768]{3,2,1,0:T(8,128)(2,1)}, u32[]{:S(2)}, u32[]{:S(2)}) collective-permute-start(bf16[1,2,128,768]{3,2,1,0:T(8,128)(2,1)S(1)} %collective-permute-done.1), channel_id=1, source_target_pairs={{0,4},{4,8},{8,12},{12,16},{16,20},{20,24},{24,28},{28,0},{1,5},{5... | collective-permute-start | bytes 1179656 | tf_op jit(solution)/shard_map/ppermute | solution.py:27
  86.4 18.4 %collective-permute-start.4 = (bf16[1,2,128,768]{3,2,1,0:T(8,128)(2,1)}, bf16[1,2,128,768]{3,2,1,0:T(8,128)(2,1)}, u32[]{:S(2)}, u32[]{:S(2)}) collective-permute-start(bf16[1,2,128,768]{3,2,1,0:T(8,128)(2,1)} %collective-permute-done.2), channel_id=1, source_target_pairs={{0,28},{4,0},{8,4},{12,8},{16,12},{20,16},{24,20},{28,24},{1,29},{... | collective-permute-start | bytes 1179656 | tf_op jit(solution)/shard_map/ppermute | solution.py:32
  100.5 18.0 %collective-permute-start.5 = (bf16[1,2,128,768]{3,2,1,0:T(8,128)(2,1)}, bf16[1,2,128,768]{3,2,1,0:T(8,128)(2,1)}, u32[]{:S(2)}, u32[]{:S(2)}) collective-permute-start(bf16[1,2,128,768]{3,2,1,0:T(8,128)(2,1)} %collective-permute-done.3), channel_id=1, source_target_pairs={{0,4},{4,8},{8,12},{12,16},{16,20},{20,24},{24,28},{28,0},{1,5},{5... | collective-permute-start | bytes 1179656 | tf_op jit(solution)/shard_map/ppermute | solution.py:27
  104.8 18.8 %collective-permute-start.6 = (bf16[1,2,128,768]{3,2,1,0:T(8,128)(2,1)}, bf16[1,2,128,768]{3,2,1,0:T(8,128)(2,1)S(1)}, u32[]{:S(2)}, u32[]{:S(2)}) collective-permute-start(bf16[1,2,128,768]{3,2,1,0:T(8,128)(2,1)} %collective-permute-done.4), channel_id=1, source_target_pairs={{0,28},{4,0},{8,4},{12,8},{16,12},{20,16},{24,20},{28,24},{1,29},{... | collective-permute-start | bytes 1179656 | tf_op jit(solution)/shard_map/ppermute | solution.py:32
  118.4 13.6 %collective-permute-start.7 = (bf16[1,2,128,768]{3,2,1,0:T(8,128)(2,1)}, bf16[1,2,128,768]{3,2,1,0:T(8,128)(2,1)S(1)}, u32[]{:S(2)}, u32[]{:S(2)}) collective-permute-start(bf16[1,2,128,768]{3,2,1,0:T(8,128)(2,1)} %collective-permute-done.5), channel_id=1, source_target_pairs={{0,4},{4,8},{8,12},{12,16},{16,20},{20,24},{24,28},{28,0},{1,5},{5... | collective-permute-start | bytes 1179656 | tf_op jit(solution)/shard_map/ppermute | solution.py:27
  132.1 6.7 %copy-start = (bf16[2,4,2,128,768]{4,3,2,1,0:T(8,128)(2,1)}, bf16[2,4,2,128,768]{4,3,2,1,0:T(8,128)(2,1)S(1)}, u32[]{:S(2)}) copy-start(bf16[2,4,2,128,768]{4,3,2,1,0:T(8,128)(2,1)S(1)} %get-tuple-element.432) | copy-start | bytes 9437188 | tf_op jit(solution)/shard_map/while
  140.5 29.1 %copy-start.3 = (bf16[768,256]{1,0:T(8,128)(2,1)S(1)}, bf16[768,256]{1,0:T(8,128)(2,1)}, u32[]{:S(2)}) copy-start(bf16[768,256]{1,0:T(8,128)(2,1)} %get-tuple-element.433) | copy-start | bytes 1179652 | tf_op jit(solution)/shard_map/while
  173.6 3.4 %copy-start.1 = (bf16[2,4,2,128,768]{4,3,2,1,0:T(8,128)(2,1)S(1)}, bf16[2,4,2,128,768]{4,3,2,1,0:T(8,128)(2,1)}, u32[]{:S(2)}) copy-start(bf16[2,4,2,128,768]{4,3,2,1,0:T(8,128)(2,1)} %copy-done) | copy-start | bytes 9437188 | tf_op jit(solution)/shard_map/while
  177.0 6.7 %copy-start = (bf16[2,4,2,128,768]{4,3,2,1,0:T(8,128)(2,1)}, bf16[2,4,2,128,768]{4,3,2,1,0:T(8,128)(2,1)S(1)}, u32[]{:S(2)}) copy-start(bf16[2,4,2,128,768]{4,3,2,1,0:T(8,128)(2,1)S(1)} %get-tuple-element.432) | copy-start | bytes 9437188 | tf_op jit(solution)/shard_map/while
  185.4 29.1 %copy-start.3 = (bf16[768,256]{1,0:T(8,128)(2,1)S(1)}, bf16[768,256]{1,0:T(8,128)(2,1)}, u32[]{:S(2)}) copy-start(bf16[768,256]{1,0:T(8,128)(2,1)} %get-tuple-element.433) | copy-start | bytes 1179652 | tf_op jit(solution)/shard_map/while
  218.5 3.4 %copy-start.1 = (bf16[2,4,2,128,768]{4,3,2,1,0:T(8,128)(2,1)S(1)}, bf16[2,4,2,128,768]{4,3,2,1,0:T(8,128)(2,1)}, u32[]{:S(2)}) copy-start(bf16[2,4,2,128,768]{4,3,2,1,0:T(8,128)(2,1)} %copy-done) | copy-start | bytes 9437188 | tf_op jit(solution)/shard_map/while
  221.9 6.7 %copy-start = (bf16[2,4,2,128,768]{4,3,2,1,0:T(8,128)(2,1)}, bf16[2,4,2,128,768]{4,3,2,1,0:T(8,128)(2,1)S(1)}, u32[]{:S(2)}) copy-start(bf16[2,4,2,128,768]{4,3,2,1,0:T(8,128)(2,1)S(1)} %get-tuple-element.432) | copy-start | bytes 9437188 | tf_op jit(solution)/shard_map/while
  230.3 29.1 %copy-start.3 = (bf16[768,256]{1,0:T(8,128)(2,1)S(1)}, bf16[768,256]{1,0:T(8,128)(2,1)}, u32[]{:S(2)}) copy-start(bf16[768,256]{1,0:T(8,128)(2,1)} %get-tuple-element.433) | copy-start | bytes 1179652 | tf_op jit(solution)/shard_map/while
  263.3 3.4 %copy-start.1 = (bf16[2,4,2,128,768]{4,3,2,1,0:T(8,128)(2,1)S(1)}, bf16[2,4,2,128,768]{4,3,2,1,0:T(8,128)(2,1)}, u32[]{:S(2)}) copy-start(bf16[2,4,2,128,768]{4,3,2,1,0:T(8,128)(2,1)} %copy-done) | copy-start | bytes 9437188 | tf_op jit(solution)/shard_map/while
  266.7 6.7 %copy-start = (bf16[2,4,2,128,768]{4,3,2,1,0:T(8,128)(2,1)}, bf16[2,4,2,128,768]{4,3,2,1,0:T(8,128)(2,1)S(1)}, u32[]{:S(2)}) copy-start(bf16[2,4,2,128,768]{4,3,2,1,0:T(8,128)(2,1)S(1)} %get-tuple-element.432) | copy-start | bytes 9437188 | tf_op jit(solution)/shard_map/while
  275.1 29.1 %copy-start.3 = (bf16[768,256]{1,0:T(8,128)(2,1)S(1)}, bf16[768,256]{1,0:T(8,128)(2,1)}, u32[]{:S(2)}) copy-start(bf16[768,256]{1,0:T(8,128)(2,1)} %get-tuple-element.433) | copy-start | bytes 1179652 | tf_op jit(solution)/shard_map/while
  308.2 3.4 %copy-start.1 = (bf16[2,4,2,128,768]{4,3,2,1,0:T(8,128)(2,1)S(1)}, bf16[2,4,2,128,768]{4,3,2,1,0:T(8,128)(2,1)}, u32[]{:S(2)}) copy-start(bf16[2,4,2,128,768]{4,3,2,1,0:T(8,128)(2,1)} %copy-done) | copy-start | bytes 9437188 | tf_op jit(solution)/shard_map/while
Sparse Core Ops, SparseCore 0:
  64.1 51.9 all-gather.2
